TPU v7x, 32 devices: a whole 2x2x4 slice. The times are simulated.
32 devices in a mesh: cell: 4 (over y, x), blk: 8 (over z, core).
Axes of the slice: x: 2, y: 2, z: 4, core: 2. Of those that a mesh axis runs over, the one named last changes fastest.
Arguments:
- codes: bfloat16 [16384, 128], P(('cell', 'blk')), may hold values from -60 to 60
- scales: float32 [16384], P(('cell', 'blk')), may hold values from 0.5 to 2
- coarse_ids: int32 [16384], P(('cell', 'blk')), may hold values from 0 to 3, as said below
- centroids: bfloat16 [32768, 128], P(('cell', 'blk')), may hold values from -6 to 6
Outputs:
- reconstruction: bfloat16 [16384, 128], P(('cell', 'blk'))
- residual: bfloat16 [16384, 128], P(('cell', 'blk'))
Inputs may be any that keep to these rules, and one draw needn't show every extreme that they name: `coarse_ids`: on every device, the number of its 512 rows that name partition g is the same for all devices; at most 256 rows of one device name one partition, and one partition is named by exactly 256 rows of every device.
All inputs are finite; a program needn't handle non-finite values.
Results may differ from a plain program's by a relative error of at most 0.006.
Values may be sent and summed in bfloat16 or wider, within the bound.
No kernel may reach another device: no remote copies, remote signals or barrier semaphores. Data moves between devices by JAX's collectives and lax.ppermute only.
A program may use at most 256 MiB of HBM per device.

v0:
```python
import math
import jax
import jax.numpy as jnp
from jax import lax
from jax.sharding import PartitionSpec as P


def local(codes, scales, coarse_ids, centroids):
    rows_dev = codes.shape[0]
    width = codes.shape[1]
    loops = lax.axis_size("cell")
    cap = 2 * rows_dev // loops
    beta = 1.0 / math.sqrt(width)
    dequant = (codes.astype(jnp.float32) * scales[:, None]).astype(jnp.bfloat16)
    onehot = (coarse_ids[:, None] == jnp.arange(loops, dtype=jnp.int32)[None, :]).astype(jnp.int32)
    ranks = jnp.sum(jnp.cumsum(onehot, axis=0) * onehot, axis=1) - 1
    slots = coarse_ids * cap + ranks
    outgoing = jnp.zeros((loops * cap, width), jnp.bfloat16).at[slots].set(dequant)
    arrived = lax.all_to_all(
        outgoing.reshape(loops, cap, width), "cell", split_axis=0, concat_axis=0, tiled=True
    )
    queries = arrived.reshape(loops * cap, width)

    def scores_of(piece):
        product = lax.dot_general(
            queries, piece, (((1,), (1,)), ((), ())), preferred_element_type=jnp.float32
        )
        return product * beta

    top = jnp.max(scores_of(lax.all_gather(centroids, "blk", axis=0, tiled=True)), axis=1)
    piece = lax.all_gather(centroids, "blk", axis=0, tiled=True)
    weights = jnp.exp(scores_of(piece) - top[:, None]).astype(jnp.bfloat16)
    total = jnp.sum(weights.astype(jnp.float32), axis=1)
    numer = jnp.dot(weights, piece, preferred_element_type=jnp.float32)
    total, numer = (total, numer)
    recon = (numer / total[:, None]).astype(jnp.bfloat16)
    remote_residual = (queries.astype(jnp.float32) - recon.astype(jnp.float32)).astype(jnp.bfloat16)
    stacked = jnp.stack([recon, remote_residual]).reshape(2, loops, cap, width)
    back = lax.all_to_all(stacked, "cell", split_axis=1, concat_axis=1, tiled=True).reshape(
        2, loops * cap, width
    )
    return (back[0][slots], back[1][slots])


def solution(mesh):
    in_specs = (
        P(("cell", "blk"), None),
        P(("cell", "blk")),
        P(("cell", "blk")),
        P(("cell", "blk"), None),
    )
    out_specs = (P(("cell", "blk"), None), P(("cell", "blk"), None))
    return jax.shard_map(local, mesh=mesh, in_specs=in_specs, out_specs=out_specs, check_vma=False)
```

profile of v0, /device:TPU:0, one launch (start us, length us, event | category | flops | bytes accessed | tf_op | source)
XLA Modules:
  0.0 99.3 jit_solution(16947095340633523881)
XLA Ops:
  7.2 0.0 all-gather.2.cloned.1.call-start
  7.2 0.7 all-gather.2.cloned.1.call-update
  7.9 0.7 fusion.6
  8.6 1.2 %reduce-window.6 = s32[4,4,128]{2,1,0:T(4,128)S(1)} reduce-window(s32[4,4,128]{2,1,0:T(4,128)S(1)} %fusion.6, s32[]{:T(128)} %constant.4.clone.1), window={size=1x1x128 pad=0_0x0_0x127_0}, to_apply=%region_0.0 | reduce-window | flops 260096 | bytes 16388 | tf_op jit(solution)/shard_map/reduce-window
  9.8 0.2 slice_reduce_fusion
  10.0 0.2 reduce-window.9
  10.2 0.1 add_bitcast_fusion
  10.3 0.7 fusion.5
  11.0 0.7 compare_select_fusion
  11.7 2.3 %scatter_custom_fusion = bf16[1024,128]{1,0:T(8,128)(2,1)S(1)} fusion(s32[512]{0:T(512)S(1)} %compare_select_fusion, bf16[512,128]{1,0:T(8,128)(2,1)} %param.4, f32[512]{0:T(512)} %param.5, bf16[]{:T(256)} %constant.8.clone.1), kind=kCustom, calls=%fused_computation.11 | custom fusion | flops 196608 | bytes 395266 | tf_op jit(solution)/shard_map/scatter | solution.py:18
  14.0 10.7 %all_to_all.10 = bf16[4,256,128]{2,1,0:T(8,128)(2,1)S(1)} all-to-all(bf16[4,256,128]{2,1,0:T(8,128)(2,1)S(1)} %bitcast.34), channel_id=1, replica_groups=mesh['cell'=4,'blk'=8] {'cell'}, dimensions={0} | all-to-all | bytes 524288 | tf_op jit(solution)/shard_map/all_to_all | solution.py:19
  24.7 16.8 %all-gather.2.cloned.1.call-done = bf16[8192,128]{1,0:T(8,128)(2,1)} async-done(((bf16[1024,128]{1,0:T(8,128)(2,1)}), bf16[8192,128]{1,0:T(8,128)(2,1)}) %all-gather.2.cloned.1.call-update) | async-done | bytes 2097168 | tf_op jit(solution)/shard_map/all_gather | solution.py:31
  41.5 14.6 %multiply_reduce_fusion = (f32[1024]{0:T(1024)S(1)}, f32[1024,8192]{1,0:T(8,128)}) fusion(bf16[1024,128]{1,0:T(8,128)(2,1)S(1)} %bitcast.33, bf16[8192,128]{1,0:T(8,128)(2,1)} %all-gather.2.cloned.1.call-done), kind=kOutput, calls=%fused_computation.5 | convolution fusion | flops 2164259840 | bytes 35917824 | tf_op jit(solution)/shard_map/dot_general | solution.py:25
  56.1 0.0 copy-start
  56.1 15.0 %convert_reduce_fusion = (f32[1024]{0:T(1024)S(1)}, bf16[1024,8192]{1,0:T(8,128)(2,1)S(1)}) fusion(f32[1024]{0:T(1024)S(1)} %get-tuple-element.6, f32[1024,8192]{1,0:T(8,128)} %get-tuple-element.7), kind=kLoop, calls=%fused_computation.3 | loop fusion | flops 41942016 | bytes 50339840 | tf_op jit(solution)/shard_map/reduce_sum | solution.py:33
  71.1 0.0 copy-done
  71.1 4.5 %subtract_convert_fusion = (bf16[1024,128]{1,0:T(8,128)(2,1)S(1)}, bf16[1024,128]{1,0:T(8,128)(2,1)S(1)}) fusion(bf16[4,256,128]{2,1,0:T(8,128)(2,1)S(1)} %all_to_all.10, f32[1024]{0:T(1024)S(1)} %get-tuple-element.2, bf16[1024,8192]{1,0:T(8,128)(2,1)S(1)} %get-tuple-element.3, bf16[8192,128]{1,0:T(8,128)(2,1)S(1)} %copy-done), kind=kOutput, calls=%fused_computation.9 | convolution fusion | flops 2148270080 | bytes 19664896 | tf_op jit(solution)/shard_map/dot_general | solution.py:34
  75.6 0.8 pad_maximum_fusion
  76.4 3.6 %all-to-all-start.1 = ((bf16[2,4,256,128]{3,2,0,1:T(8,128)(2,1)}), bf16[2,4,256,128]{3,2,0,1:T(8,128)(2,1)S(1)}, u32[]{:S(2)}, u32[]{:S(2)}) async-start(bf16[2,4,256,128]{3,2,0,1:T(8,128)(2,1)} %pad_maximum_fusion), calls=%async_computation.1 | async-start | bytes 1048576 | tf_op jit(solution)/shard_map/all_to_all | solution.py:39
  80.1 8.5 %all-to-all-done.1 = bf16[2,4,256,128]{3,2,0,1:T(8,128)(2,1)S(1)} async-done(((bf16[2,4,256,128]{3,2,0,1:T(8,128)(2,1)}), bf16[2,4,256,128]{3,2,0,1:T(8,128)(2,1)S(1)}, u32[]{:S(2)}, u32[]{:S(2)}) %all-to-all-start.1) | async-done | bytes 524320 | tf_op jit(solution)/shard_map/all_to_all | solution.py:39
  88.6 1.9 %gather_fusion.1 = bf16[512,128]{1,0:T(8,128)(2,1)} fusion(bf16[1024,128]{1,0:T(8,128)(2,1)S(1)} %bitcast.32, s32[1024]{0:T(1024)S(1)} %pad_clamp_fusion), kind=kCustom, calls=%fused_computation.1 | custom fusion | bytes 264192 | tf_op jit(solution)/shard_map/gather | solution.py:42
  90.5 1.9 %gather_fusion = bf16[512,128]{1,0:T(8,128)(2,1)} fusion(bf16[1024,128]{1,0:T(8,128)(2,1)S(1)} %bitcast.31, s32[1024]{0:T(1024)S(1)} %pad_clamp_fusion), kind=kCustom, calls=%fused_computation | custom fusion | bytes 264192 | tf_op jit(solution)/shard_map/gather | solution.py:42
  (2 shorter events, 0.0 us)
Async XLA Ops:
  7.2 34.3 %all-gather.2.cloned.1.call-start = ((), (), s32[]{:S(2)}) async-start(), calls=%async_computation.2 | async-start | bytes 2359296 | tf_op jit(solution)/shard_map/all_gather | solution.py:31
  56.1 15.0 %copy-start = (bf16[8192,128]{1,0:T(8,128)(2,1)S(1)}, bf16[8192,128]{1,0:T(8,128)(2,1)}, u32[]{:S(2)}) copy-start(bf16[8192,128]{1,0:T(8,128)(2,1)} %all-gather.2.cloned.1.call-done) | copy-start | bytes 6291460
  76.4 12.1 %all-to-all-start.1 = ((bf16[2,4,256,128]{3,2,0,1:T(8,128)(2,1)}), bf16[2,4,256,128]{3,2,0,1:T(8,128)(2,1)S(1)}, u32[]{:S(2)}, u32[]{:S(2)}) async-start(bf16[2,4,256,128]{3,2,0,1:T(8,128)(2,1)} %pad_maximum_fusion), calls=%async_computation.1 | async-start | bytes 1048576 | tf_op jit(solution)/shard_map/all_to_all | solution.py:39
Sparse Core Ops, SparseCore 0:
  9.6 31.8 all-gather.1
where the time goes:
time: 99.7 us; the launch traced here: 99.3 us
  waiting for transfers between devices  26 us (26%)
  other arithmetic  21.6 us (22%)
  matrix products  19.1 us (19%)
  between operations  14.1 us (14%)
  blocking collectives  10.7 us (11%)
  local copies, waits for them, and re-layouts  4.08 us (4%)
  starting transfers between devices  3.69 us (4%)
    all_gather x1, waiting for transfers between devices, local(): piece = lax.all_gather(centroids, 'blk', axis=0, tiled=True)  16.8 us
    reduce_sum x1, other arithmetic, local(): total = jnp.sum(weights.astype(jnp.float32), axis=1)  15 us
    dot_general x1, matrix products, scores_of(): lax.dot_general(queries, piece, (((1,), (1,)), ((), ())), preferred_eleme...  14.6 us
    all_to_all x1, blocking collectives, local(): lax.all_to_all(outgoing.reshape(loops, cap, width), 'cell', split_axis=0,...  10.7 us
    all_to_all x1, waiting for transfers between devices, local(): lax.all_to_all(stacked, 'cell', split_axis=1, concat_axis=1, tiled=True)  8.47 us
    dot_general x1, matrix products, local(): numer = jnp.dot(weights, piece, preferred_element_type=jnp.float32)  4.49 us
    gather x2, local copies, waits for them, and re-layouts, local(): return (back[0][slots], back[1][slots])  3.83 us
    all_to_all x1, starting transfers between devices, local(): lax.all_to_all(stacked, 'cell', split_axis=1, concat_axis=1, tiled=True)  3.65 us
  transfers between devices with their start and end apart: 2, of which 2 were waited for; matrix products, arithmetic and copies ran while one was open for 6% of the time, Pallas kernels for 0%

commit v1 on v0

--- a/solution.py
+++ b/solution.py
@@ -28,7 +28,22 @@
         return product * beta
 
     top = jnp.max(scores_of(lax.all_gather(centroids, "blk", axis=0, tiled=True)), axis=1)
-    piece = lax.all_gather(centroids, "blk", axis=0, tiled=True)
+    size, index, rows = (lax.axis_size("blk"), lax.axis_index("blk"), centroids.shape[0])
+    upward = [(i, (i + 1) % size) for i in range(size)]
+    left = [(i, (i - 1) % size) for i in range(size)]
+    out = jnp.zeros((*centroids.shape[:0], size * rows, *centroids.shape[0 + 1 :]), centroids.dtype)
+    out = lax.dynamic_update_slice_in_dim(out, centroids, index * rows, axis=0)
+    from_left = from_right = centroids
+    middle = size // 2
+    for step in range(1, middle + 1):
+        from_left = lax.ppermute(from_left, "blk", upward)
+        out = lax.dynamic_update_slice_in_dim(out, from_left, (index - step) % size * rows, axis=0)
+        if step < size - middle:
+            from_right = lax.ppermute(from_right, "blk", left)
+            out = lax.dynamic_update_slice_in_dim(
+                out, from_right, (index + step) % size * rows, axis=0
+            )
+    piece = out
     weights = jnp.exp(scores_of(piece) - top[:, None]).astype(jnp.bfloat16)
     total = jnp.sum(weights.astype(jnp.float32), axis=1)
     numer = jnp.dot(weights, piece, preferred_element_type=jnp.float32)

time: 99.7 us -> 104 us (1.043)
  starting transfers between devices: 3.69 us -> 23.1 us
  other arithmetic: 21.6 us -> 7.29 us
  blocking collectives: 10.7 us -> 0 us
  matrix products: 19.1 us -> 26 us
  waiting for transfers between devices: 26 us -> 28.8 us
    ppermute x0 -> x7, waiting for transfers between devices: none -> 19.2 us  [the longest x3 12 us: local(): from_right = lax.ppermute(from_right, 'blk', left)]
    all_gather x1, waiting for transfers between devices: 16.8 us -> 0.02 us  [local(): lax.all_gather(centroids, 'blk', axis=0, tiled=True)]
    reduce_sum x1 -> x0, other arithmetic: 15 us -> none  [local(): total = jnp.sum(weights.astype(jnp.float32), axis=1)]
    ppermute x0 -> x7, starting transfers between devices: none -> 13.8 us  [the longest x3 11.1 us: local(): from_right = lax.ppermute(from_right, 'blk', left)]
    all_to_all x1 -> x0, blocking collectives: 10.7 us -> none  [local(): lax.all_to_all(outgoing.reshape(loops, cap, width), 'cell', split_axis=0,...]
    all_to_all x0 -> x1, starting transfers between devices: none -> 4.72 us  [local(): lax.all_to_all(outgoing.reshape(loops, cap, width), 'cell', split_axis=0,...]
    dot_general x1, matrix products: 4.49 us -> 8.4 us  [local(): numer = jnp.dot(weights, piece, preferred_element_type=jnp.float32)]
    dot_general x1 -> x2, matrix products: 14.6 us -> 17.6 us  [scores_of(): lax.dot_general(queries, piece, (((1,), (1,)), ((), ())), preferred_eleme...]
  transfers between devices with their start and end apart: 2 -> 10, of which waited for: 2 -> 6; matrix products, arithmetic and copies ran while one was open for 6% -> 7% of each run, Pallas kernels for 0% -> 0%
where the time goes in v1:
time: 104 us
  waiting for transfers between devices  28.8 us (28%)
  matrix products  26 us (25%)
  starting transfers between devices  23.1 us (22%)
  between operations  14.3 us (14%)
  other arithmetic  7.29 us (7%)
  local copies, waits for them, and re-layouts  4.66 us (4%)
    dot_general x2, matrix products, scores_of(): lax.dot_general(queries, piece, (((1,), (1,)), ((), ())), preferred_eleme...  17.6 us
    ppermute x3, waiting for transfers between devices, local(): from_right = lax.ppermute(from_right, 'blk', left)  12 us
    ppermute x3, starting transfers between devices, local(): from_right = lax.ppermute(from_right, 'blk', left)  11.1 us
    all_to_all x1, waiting for transfers between devices, local(): lax.all_to_all(stacked, 'cell', split_axis=1, concat_axis=1, tiled=True)  8.87 us
    dot_general x1, matrix products, local(): numer = jnp.dot(weights, piece, preferred_element_type=jnp.float32)  8.4 us
    ppermute x4, waiting for transfers between devices, local(): from_left = lax.ppermute(from_left, 'blk', upward)  7.2 us
    all_to_all x1, starting transfers between devices, local(): lax.all_to_all(outgoing.reshape(loops, cap, width), 'cell', split_axis=0,...  4.72 us
    all_to_all x1, starting transfers between devices, local(): lax.all_to_all(stacked, 'cell', split_axis=1, concat_axis=1, tiled=True)  4.5 us
  transfers between devices with their start and end apart: 10, of which 6 were waited for; matrix products, arithmetic and copies ran while one was open for 7% of the time, Pallas kernels for 0%

profile of v1, /device:TPU:0, one launch (start us, length us, event | category | flops | bytes accessed | tf_op | source)
XLA Modules:
  0.0 104.1 jit_solution(3592805443682109278)
XLA Ops:
  7.2 0.0 copy-start
  7.2 0.0 all-gather.2.cloned.1.call-start
  7.2 0.7 all-gather.2.cloned.1.call-update
  7.9 0.5 collective-permute-start
  8.5 4.1 %collective-permute-start.1 = (bf16[1024,128]{1,0:T(8,128)(2,1)}, bf16[1024,128]{1,0:T(8,128)(2,1)S(1)}, u32[]{:S(2)}, u32[]{:S(2)}) collective-permute-start(bf16[1024,128]{1,0:T(8,128)(2,1)} %param.7), channel_id=1, source_target_pairs={{0,7},{1,0},{2,1},{3,2},{4,3},{5,4},{6,5},{7,6},{8,15},{9,8},{10,9... | collective-permute-start | bytes 786440 | tf_op jit(solution)/shard_map/ppermute | solution.py:42
  12.5 0.7 fusion.6
  13.2 1.2 %reduce-window.6 = s32[4,4,128]{2,1,0:T(4,128)S(1)} reduce-window(s32[4,4,128]{2,1,0:T(4,128)S(1)} %fusion.6, s32[]{:T(128)} %constant.64.clone.1), window={size=1x1x128 pad=0_0x0_0x127_0}, to_apply=%region_0.0 | reduce-window | flops 260096 | bytes 16388 | tf_op jit(solution)/shard_map/reduce-window
  14.4 0.2 slice_reduce_fusion
  14.7 0.2 reduce-window.9
  14.8 0.1 add_bitcast_fusion
  14.9 0.7 fusion.5
  15.6 1.3 %collective-permute-done = bf16[1024,128]{1,0:T(8,128)(2,1)S(1)} collective-permute-done((bf16[1024,128]{1,0:T(8,128)(2,1)}, bf16[1024,128]{1,0:T(8,128)(2,1)S(1)}, u32[]{:S(2)}, u32[]{:S(2)}) %collective-permute-start) | collective-permute-done | bytes 262176 | tf_op jit(solution)/shard_map/ppermute | solution.py:39
  17.0 0.0 collective-permute-start.2
  17.0 0.7 compare_select_fusion
  17.6 2.9 %scatter_custom_fusion = bf16[1024,128]{1,0:T(8,128)(2,1)} fusion(s32[512]{0:T(512)S(1)} %compare_select_fusion, bf16[512,128]{1,0:T(8,128)(2,1)} %param.4, f32[512]{0:T(512)} %param.5, bf16[]{:T(256)} %constant.62.clone.1), kind=kCustom, calls=%fused_computation.11 | custom fusion | flops 196608 | bytes 395266 | tf_op jit(solution)/shard_map/scatter | solution.py:18
  20.6 4.7 %all-to-all-start = ((bf16[4,256,128]{2,1,0:T(8,128)(2,1)}), bf16[4,256,128]{2,1,0:T(8,128)(2,1)}, u32[]{:S(2)}, u32[]{:S(2)}) async-start(bf16[4,256,128]{2,1,0:T(8,128)(2,1)} %bitcast.2), calls=%async_computation | async-start | bytes 524288 | tf_op jit(solution)/shard_map/all_to_all | solution.py:19
  25.3 0.0 collective-permute-done.1
  25.3 3.3 %collective-permute-start.3 = (bf16[1024,128]{1,0:T(8,128)(2,1)S(1)}, bf16[1024,128]{1,0:T(8,128)(2,1)S(1)}, u32[]{:S(2)}, u32[]{:S(2)}) collective-permute-start(bf16[1024,128]{1,0:T(8,128)(2,1)S(1)} %collective-permute-done.1), channel_id=1, source_target_pairs={{0,7},{1,0},{2,1},{3,2},{4,3},{5,4},{6,5},{7,6},{8,15},{9,8},{10,9... | collective-permute-start | bytes 786440 | tf_op jit(solution)/shard_map/ppermute | solution.py:42
  28.5 0.3 broadcast_in_dim.8
  28.8 0.0 copy-done
  29.0 0.0 collective-permute-done.2
  29.0 0.1 collective-permute-start.4
  29.2 11.0 %collective-permute-done.3 = bf16[1024,128]{1,0:T(8,128)(2,1)S(1)} collective-permute-done((bf16[1024,128]{1,0:T(8,128)(2,1)S(1)}, bf16[1024,128]{1,0:T(8,128)(2,1)S(1)}, u32[]{:S(2)}, u32[]{:S(2)}) %collective-permute-start.3) | collective-permute-done | bytes 262176 | tf_op jit(solution)/shard_map/ppermute | solution.py:42
  40.2 3.8 %collective-permute-start.5 = (bf16[1024,128]{1,0:T(8,128)(2,1)S(1)}, bf16[1024,128]{1,0:T(8,128)(2,1)S(1)}, u32[]{:S(2)}, u32[]{:S(2)}) collective-permute-start(bf16[1024,128]{1,0:T(8,128)(2,1)S(1)} %collective-permute-done.3), channel_id=1, source_target_pairs={{0,7},{1,0},{2,1},{3,2},{4,3},{5,4},{6,5},{7,6},{8,15},{9,8},{10,9... | collective-permute-start | bytes 786440 | tf_op jit(solution)/shard_map/ppermute | solution.py:42
  44.0 0.8 collective-permute-done.4
  44.8 2.1 %collective-permute-start.6 = (bf16[1024,128]{1,0:T(8,128)(2,1)S(1)}, bf16[1024,128]{1,0:T(8,128)(2,1)S(1)}, u32[]{:S(2)}, u32[]{:S(2)}) collective-permute-start(bf16[1024,128]{1,0:T(8,128)(2,1)S(1)} %collective-permute-done.4), channel_id=1, source_target_pairs={{0,1},{1,2},{2,3},{3,4},{4,5},{5,6},{6,7},{7,0},{8,9},{9,10},{10,1... | collective-permute-start | bytes 786440 | tf_op jit(solution)/shard_map/ppermute | solution.py:39
  47.0 0.9 collective-permute-done.5
  47.9 5.1 %collective-permute-done.6 = bf16[1024,128]{1,0:T(8,128)(2,1)S(1)} collective-permute-done((bf16[1024,128]{1,0:T(8,128)(2,1)S(1)}, bf16[1024,128]{1,0:T(8,128)(2,1)S(1)}, u32[]{:S(2)}, u32[]{:S(2)}) %collective-permute-start.6) | collective-permute-done | bytes 262176 | tf_op jit(solution)/shard_map/ppermute | solution.py:39
  53.1 0.0 all-to-all-done
  53.1 0.0 all-gather.2.cloned.1.call-done
  53.1 6.3 %multiply_reduce_fusion = f32[1024]{0:T(1024)S(1)} fusion(bf16[1024,128]{1,0:T(8,128)(2,1)} %bitcast.3, bf16[8192,128]{1,0:T(8,128)(2,1)} %all-gather.2.cloned.1.call-done), kind=kOutput, calls=%fused_computation.5 | convolution fusion | flops 2164259840 | bytes 2363392 | tf_op jit(solution)/shard_map/dot_general | solution.py:25
  59.4 11.3 %convert_reduce_fusion = (f32[1024]{0:T(1024)S(1)}, bf16[1024,8192]{1,0:T(8,128)(2,1)}) fusion(f32[1024]{0:T(1024)S(1)} %multiply_reduce_fusion, bf16[1024,128]{1,0:T(8,128)(2,1)} %bitcast.3, bf16[8192,128]{1,0:T(8,128)(2,1)S(1)} %constant_dynamic-update-slice_fusion), kind=kOutput, calls=%fused_computation.3 | convolution fusion | flops 2189425664 | bytes 19144704 | tf_op jit(solution)/shard_map/dot_general | solution.py:25
  70.7 8.4 %subtract_convert_fusion = (bf16[1024,128]{1,0:T(8,128)(2,1)S(1)}, bf16[1024,128]{1,0:T(8,128)(2,1)S(1)}) fusion(bf16[4,256,128]{2,1,0:T(8,128)(2,1)} %all-to-all-done, f32[1024]{0:T(1024)S(1)} %get-tuple-element.4, bf16[1024,8192]{1,0:T(8,128)(2,1)} %get-tuple-element.5, bf16[8192,128]{1,0:T(8,128)(2,1)S(1)} %constant_dynamic-update-slice_fusion), kind=kOutput, calls=%fused_computation.9 | convolution fusion | flops 2148270080 | bytes 19664896 | tf_op jit(solution)/shard_map/dot_general | solution.py:49
  79.1 0.8 pad_maximum_fusion
  80.0 4.5 %all-to-all-start.1 = ((bf16[2,4,256,128]{3,2,0,1:T(8,128)(2,1)}), bf16[2,4,256,128]{3,2,0,1:T(8,128)(2,1)S(1)}, u32[]{:S(2)}, u32[]{:S(2)}) async-start(bf16[2,4,256,128]{3,2,0,1:T(8,128)(2,1)} %pad_maximum_fusion), calls=%async_computation.1 | async-start | bytes 1048576 | tf_op jit(solution)/shard_map/all_to_all | solution.py:54
  84.5 8.9 %all-to-all-done.1 = bf16[2,4,256,128]{3,2,0,1:T(8,128)(2,1)S(1)} async-done(((bf16[2,4,256,128]{3,2,0,1:T(8,128)(2,1)}), bf16[2,4,256,128]{3,2,0,1:T(8,128)(2,1)S(1)}, u32[]{:S(2)}, u32[]{:S(2)}) %all-to-all-start.1) | async-done | bytes 524320 | tf_op jit(solution)/shard_map/all_to_all | solution.py:54
  93.4 1.9 %gather_fusion.1 = bf16[512,128]{1,0:T(8,128)(2,1)} fusion(bf16[1024,128]{1,0:T(8,128)(2,1)S(1)} %bitcast.34, s32[1024]{0:T(1024)S(1)} %pad_clamp_fusion), kind=kCustom, calls=%fused_computation.1 | custom fusion | bytes 264192 | tf_op jit(solution)/shard_map/gather | solution.py:57
  95.3 1.9 %gather_fusion = bf16[512,128]{1,0:T(8,128)(2,1)} fusion(bf16[1024,128]{1,0:T(8,128)(2,1)S(1)} %bitcast.33, s32[1024]{0:T(1024)S(1)} %pad_clamp_fusion), kind=kCustom, calls=%fused_computation | custom fusion | bytes 264192 | tf_op jit(solution)/shard_map/gather | solution.py:57
  (10 shorter events, 0.3 us)
Async XLA Ops:
  7.2 21.7 %copy-start = (bf16[1024,128]{1,0:T(8,128)(2,1)S(1)}, bf16[1024,128]{1,0:T(8,128)(2,1)}, u32[]{:S(2)}) copy-start(bf16[1024,128]{1,0:T(8,128)(2,1)} %param.7) | copy-start | bytes 786436
  7.2 45.9 %all-gather.2.cloned.1.call-start = ((), (), s32[]{:S(2)}) async-start(), calls=%async_computation.2 | async-start | bytes 2359296 | tf_op jit(solution)/shard_map/all_gather | solution.py:30
  7.9 9.0 %collective-permute-start = (bf16[1024,128]{1,0:T(8,128)(2,1)}, bf16[1024,128]{1,0:T(8,128)(2,1)S(1)}, u32[]{:S(2)}, u32[]{:S(2)}) collective-permute-start(bf16[1024,128]{1,0:T(8,128)(2,1)} %param.7), channel_id=1, source_target_pairs={{0,1},{1,2},{2,3},{3,4},{4,5},{5,6},{6,7},{7,0},{8,9},{9,10},{10,1... | collective-permute-start | bytes 786440 | tf_op jit(solution)/shard_map/ppermute | solution.py:39
  8.5 16.8 %collective-permute-start.1 = (bf16[1024,128]{1,0:T(8,128)(2,1)}, bf16[1024,128]{1,0:T(8,128)(2,1)S(1)}, u32[]{:S(2)}, u32[]{:S(2)}) collective-permute-start(bf16[1024,128]{1,0:T(8,128)(2,1)} %param.7), channel_id=1, source_target_pairs={{0,7},{1,0},{2,1},{3,2},{4,3},{5,4},{6,5},{7,6},{8,15},{9,8},{10,9... | collective-permute-start | bytes 786440 | tf_op jit(solution)/shard_map/ppermute | solution.py:42
  17.0 12.1 %collective-permute-start.2 = (bf16[1024,128]{1,0:T(8,128)(2,1)S(1)}, bf16[1024,128]{1,0:T(8,128)(2,1)S(1)}, u32[]{:S(2)}, u32[]{:S(2)}) collective-permute-start(bf16[1024,128]{1,0:T(8,128)(2,1)S(1)} %collective-permute-done), channel_id=1, source_target_pairs={{0,1},{1,2},{2,3},{3,4},{4,5},{5,6},{6,7},{7,0},{8,9},{9,10},{10,1... | collective-permute-start | bytes 786440 | tf_op jit(solution)/shard_map/ppermute | solution.py:39
  20.6 32.5 %all-to-all-start = ((bf16[4,256,128]{2,1,0:T(8,128)(2,1)}), bf16[4,256,128]{2,1,0:T(8,128)(2,1)}, u32[]{:S(2)}, u32[]{:S(2)}) async-start(bf16[4,256,128]{2,1,0:T(8,128)(2,1)} %bitcast.2), calls=%async_computation | async-start | bytes 524288 | tf_op jit(solution)/shard_map/all_to_all | solution.py:19
  25.3 14.9 %collective-permute-start.3 = (bf16[1024,128]{1,0:T(8,128)(2,1)S(1)}, bf16[1024,128]{1,0:T(8,128)(2,1)S(1)}, u32[]{:S(2)}, u32[]{:S(2)}) collective-permute-start(bf16[1024,128]{1,0:T(8,128)(2,1)S(1)} %collective-permute-done.1), channel_id=1, source_target_pairs={{0,7},{1,0},{2,1},{3,2},{4,3},{5,4},{6,5},{7,6},{8,15},{9,8},{10,9... | collective-permute-start | bytes 786440 | tf_op jit(solution)/shard_map/ppermute | solution.py:42
  29.0 15.8 %collective-permute-start.4 = (bf16[1024,128]{1,0:T(8,128)(2,1)S(1)}, bf16[1024,128]{1,0:T(8,128)(2,1)S(1)}, u32[]{:S(2)}, u32[]{:S(2)}) collective-permute-start(bf16[1024,128]{1,0:T(8,128)(2,1)S(1)} %collective-permute-done.2), channel_id=1, source_target_pairs={{0,1},{1,2},{2,3},{3,4},{4,5},{5,6},{6,7},{7,0},{8,9},{9,10},{10,1... | collective-permute-start | bytes 786440 | tf_op jit(solution)/shard_map/ppermute | solution.py:39
  40.2 7.7 %collective-permute-start.5 = (bf16[1024,128]{1,0:T(8,128)(2,1)S(1)}, bf16[1024,128]{1,0:T(8,128)(2,1)S(1)}, u32[]{:S(2)}, u32[]{:S(2)}) collective-permute-start(bf16[1024,128]{1,0:T(8,128)(2,1)S(1)} %collective-permute-done.3), channel_id=1, source_target_pairs={{0,7},{1,0},{2,1},{3,2},{4,3},{5,4},{6,5},{7,6},{8,15},{9,8},{10,9... | collective-permute-start | bytes 786440 | tf_op jit(solution)/shard_map/ppermute | solution.py:42
  44.8 8.2 %collective-permute-start.6 = (bf16[1024,128]{1,0:T(8,128)(2,1)S(1)}, bf16[1024,128]{1,0:T(8,128)(2,1)S(1)}, u32[]{:S(2)}, u32[]{:S(2)}) collective-permute-start(bf16[1024,128]{1,0:T(8,128)(2,1)S(1)} %collective-permute-done.4), channel_id=1, source_target_pairs={{0,1},{1,2},{2,3},{3,4},{4,5},{5,6},{6,7},{7,0},{8,9},{9,10},{10,1... | collective-permute-start | bytes 786440 | tf_op jit(solution)/shard_map/ppermute | solution.py:39
  80.0 13.4 %all-to-all-start.1 = ((bf16[2,4,256,128]{3,2,0,1:T(8,128)(2,1)}), bf16[2,4,256,128]{3,2,0,1:T(8,128)(2,1)S(1)}, u32[]{:S(2)}, u32[]{:S(2)}) async-start(bf16[2,4,256,128]{3,2,0,1:T(8,128)(2,1)} %pad_maximum_fusion), calls=%async_computation.1 | async-start | bytes 1048576 | tf_op jit(solution)/shard_map/all_to_all | solution.py:54
Sparse Core Ops, SparseCore 0:
  9.6 38.9 all-gather.1
